TPU v7x, 32 devices: a whole 2x2x4 slice. The times are simulated.
32 devices in a mesh: req: 4 (over y, x), exp: 8 (over z, core).
Axes of the slice: x: 2, y: 2, z: 4, core: 2. Of those that a mesh axis runs over, the one named last changes fastest.
Arguments:
- tokens: bfloat16 [4, 512, 2048], P('req', 'exp'), may hold values from -6 to 6
- cache: bfloat16 [4, 1024, 4096], P('req', None, 'exp'), may hold values from -64 to 64
- cache_len: int32 [4], P('req'), may hold values from 1 to 1024, 2560 in all
- attn_routes: int32 [4, 512, 2], P('req', 'exp'), may hold values from 0 to 7, all different within a row; in each aligned block of 64 rows (0 to 63, 64 to 127, ..., all dimensions but the last counted through in order) at most 24 rows name the same one
- mlp_routes: int32 [4, 512, 2], P('req', 'exp'), may hold values from 0 to 7, all different within a row; in each aligned block of 64 rows (0 to 63, 64 to 127, ..., all dimensions but the last counted through in order) at most 24 rows name the same one
- norm_attn: float32 [2048], replicated, may hold values from 0.5 to 1.5
- attn_router: bfloat16 [2048, 8], replicated, may hold values from -0.125 to 0.125
- w_query: bfloat16 [128, 2048, 128], P('exp'), may hold values from -0.125 to 0.125
- w_keyval: bfloat16 [2048, 4096], P(None, 'exp'), may hold values from -0.125 to 0.125
- w_out: bfloat16 [128, 128, 2048], P('exp'), may hold values from -0.125 to 0.125
- norm_mlp: float32 [2048], replicated, may hold values from 0.5 to 1.5
- mlp_router: bfloat16 [2048, 8], replicated, may hold values from -0.125 to 0.125
- w_gate: bfloat16 [8, 2048, 5632], P('exp'), may hold values from -0.125 to 0.125
- w_up: bfloat16 [8, 2048, 5632], P('exp'), may hold values from -0.125 to 0.125
- w_down: bfloat16 [8, 5632, 2048], P('exp'), may hold values from -0.078125 to 0.078125
Outputs:
- hidden_out: bfloat16 [4, 512, 2048], P('req', 'exp')
- cache_out: bfloat16 [4, 1536, 4096], P('req', None, 'exp')
Inputs may be any that keep to these rules, and one draw needn't show every extreme that they name: `attn_routes`: in each aligned block of 64 rows, no expert is named by more than 24 rows. `mlp_routes`: in each aligned block of 64 rows, no expert is named by more than 24 rows.
All inputs are finite; a program needn't handle non-finite values. No bound on the sum of `cache_len` on one device may be relied on, other than what follows from the above.
Results may differ from a plain program's by a relative error of at most 0.015.
The roundings to bfloat16 on the way count: a program that leaves them out, or rounds other values in their place, can miss the bound.
Values may be sent and summed in bfloat16 or wider, within the bound.
No kernel may reach another device: no remote copies, remote signals or barrier semaphores. Data moves between devices by JAX's collectives and lax.ppermute only.
A program may use at most 256 MiB of HBM per device.

v0:
```python
import math
import jax
import jax.numpy as jnp
from jax import lax
from jax.sharding import PartitionSpec as P

MOST = 24
epsilon = 1e-05
rope_base = 10000.0
masked_score = -1e30


def from_partner(value, axis, stride):
    mask = 2**stride
    pairs = [(source, source ^ mask) for source in range(lax.axis_size(axis))]
    return lax.ppermute(value, axis, pairs)


def rms_norm(values, gain_vec):
    widened = values.astype(jnp.float32)
    inv_rms = lax.rsqrt(jnp.mean(widened * widened, axis=-1, keepdims=True) + epsilon)
    return (widened * inv_rms * gain_vec).astype(jnp.bfloat16)


def rotate(values, position):
    half_dim = values.shape[-1] // 2
    inv_freq = rope_base ** (-jnp.arange(half_dim).astype(jnp.float32) / half_dim)
    angles = position.astype(jnp.float32)[..., None] * inv_freq
    cosine = jnp.cos(angles)
    sines = jnp.sin(angles)
    first_half = values[..., :half_dim]
    second_half = values[..., half_dim:]
    return jnp.concatenate(
        [first_half * cosine - second_half * sines, second_half * cosine + first_half * sines],
        axis=-1,
    )


def pick_gates(normed, router, routes):
    logits = jnp.dot(normed, router, preferred_element_type=jnp.float32)
    labels = jnp.arange(router.shape[1], dtype=jnp.int32)
    onehot = (routes[:, :, None] == labels[None, None, :]).astype(jnp.float32)
    chosen = jnp.sum(onehot * logits[:, None, :], axis=-1)
    return jax.nn.softmax(chosen, axis=-1)


def slot_tables(routes, gates, labels, rows_block, slot_count):
    row_total = routes.shape[0]
    block_count = row_total // rows_block
    matches = routes[:, :, None] == labels[None, None, :]
    member = jnp.any(matches, axis=1).astype(jnp.int32).reshape(block_count, rows_block, -1)
    weight = jnp.sum(jnp.where(matches, gates[:, :, None], 0.0), axis=1).reshape(
        block_count, rows_block, -1
    )
    ranking = jnp.cumsum(member, axis=1) - 1
    slot_ids = jnp.arange(slot_count, dtype=jnp.int32)
    onehot = ((member[..., None] > 0) & (ranking[..., None] == slot_ids)).astype(jnp.int32)
    local_row = jnp.arange(rows_block, dtype=jnp.int32)[None, :, None, None]
    token_ids = (
        jnp.sum(onehot * local_row, axis=1)
        + (jnp.arange(block_count, dtype=jnp.int32) * rows_block)[:, None, None]
    )
    shares = jnp.sum(onehot.astype(jnp.float32) * weight[..., None], axis=1)
    return (token_ids, shares)


def spread_rows(terms, token_ids, extent):
    term_part = terms.reshape(-1, terms.shape[-1])
    id_part = token_ids.reshape(-1)
    return jnp.zeros((extent, terms.shape[-1]), jnp.float32).at[id_part].add(term_part, mode="drop")


def attend(queries, query_pos, key_cache, value_cache, key_fresh, value_fresh, length):
    query_count = queries.shape[0]
    head_dim = queries.shape[1]
    factor = head_dim ** (-0.5)

    def absorb(state, key_block, value_block, visible):
        running_top, running_total, running_acc = state
        scores = jnp.dot(queries, key_block.T, preferred_element_type=jnp.float32) * factor
        scores = jnp.where(visible, scores, masked_score)
        new_top = jnp.maximum(running_top, jnp.max(scores, axis=1))
        fading = jnp.exp(running_top - new_top)
        weights = jnp.exp(scores - new_top[:, None])
        running_total = running_total * fading + jnp.sum(weights, axis=1)
        running_acc = running_acc * fading[:, None] + jnp.dot(
            weights.astype(jnp.bfloat16), value_block, preferred_element_type=jnp.float32
        )
        return (new_top, running_total, running_acc)

    state = (
        jnp.full((query_count,), masked_score, jnp.float32),
        jnp.zeros((query_count,), jnp.float32),
        jnp.zeros((query_count, head_dim), jnp.float32),
    )
    cache_span = math.gcd(512, key_cache.shape[0])

    def cache_step(step_idx, state):
        offset = step_idx * cache_span
        key_block = lax.dynamic_slice_in_dim(key_cache, offset, cache_span, 0)
        value_block = lax.dynamic_slice_in_dim(value_cache, offset, cache_span, 0)
        visible = (offset + jnp.arange(cache_span, dtype=jnp.int32))[None, :] < length
        return absorb(state, key_block, value_block, visible)

    state = lax.fori_loop(0, (length + cache_span - 1) // cache_span, cache_step, state)
    fresh_span = math.gcd(512, key_fresh.shape[0])
    for offset in range(0, key_fresh.shape[0], fresh_span):
        visible = (offset + jnp.arange(fresh_span, dtype=jnp.int32))[None, :] <= query_pos[:, None]
        state = absorb(
            state,
            key_fresh[offset : offset + fresh_span],
            value_fresh[offset : offset + fresh_span],
            visible,
        )
    running_top, running_total, running_acc = state
    return (running_acc / running_total[:, None]).astype(jnp.bfloat16)


def body(
    tokens,
    cache,
    cache_len,
    attn_routes,
    mlp_routes,
    norm_attn,
    attn_router,
    w_query,
    w_keyval,
    w_out,
    norm_mlp,
    mlp_router,
    w_gate,
    w_up,
    w_down,
):
    device_count = lax.axis_size("exp")
    position = lax.axis_index("exp")
    own_rows = tokens[0]
    rows_block = own_rows.shape[0]
    model_width = own_rows.shape[1]
    length = cache_len[0]
    slot_count = MOST
    normed = rms_norm(own_rows, norm_attn)
    group_normed, group_routes = (
        lax.all_gather(normed, "exp", axis=0, tiled=True),
        lax.all_gather(attn_routes[0], "exp", axis=0, tiled=True),
    )
    row_total = group_normed.shape[0]
    block_count = row_total // rows_block
    heads_here = w_query.shape[0]
    head_dim = w_query.shape[2]
    columns = w_keyval.shape[1]
    experts_attn = attn_router.shape[1]
    my_attn = jnp.reshape(position % experts_attn, (1,))
    new_pos = length + jnp.arange(row_total, dtype=jnp.int32)
    fresh_kv = jnp.dot(group_normed, w_keyval, preferred_element_type=jnp.float32)
    if columns < 2 * head_dim:
        is_key = position % 2 == 0
        fresh_kv = jnp.where(is_key, rotate(fresh_kv, new_pos), fresh_kv).astype(jnp.bfloat16)
    else:
        split_new = fresh_kv.reshape(row_total, columns // (2 * head_dim), 2, head_dim)
        rotated = rotate(split_new[:, :, 0], new_pos[:, None])
        fresh_kv = (
            jnp.stack([rotated, split_new[:, :, 1]], axis=2)
            .astype(jnp.bfloat16)
            .reshape(row_total, columns)
        )
    cache_limit = cache.shape[1]
    padded = jnp.concatenate([cache[0], jnp.zeros((row_total, columns), jnp.bfloat16)], axis=0)
    placed = lax.dynamic_update_slice(jnp.zeros_like(padded), fresh_kv, (length, jnp.int32(0)))
    slot_ids = jnp.arange(cache_limit + row_total, dtype=jnp.int32)
    cache_next = jnp.where((slot_ids < length)[:, None], padded, placed)
    group_cache = cache[0]
    group_fresh = fresh_kv
    for bit in range(experts_attn.bit_length() - 1):
        other_cache, other_fresh = from_partner((group_cache, group_fresh), "exp", bit)
        lower = position // (1 << bit) % 2 == 0
        group_cache = jnp.where(
            lower,
            jnp.concatenate([group_cache, other_cache], axis=1),
            jnp.concatenate([other_cache, group_cache], axis=1),
        )
        group_fresh = jnp.where(
            lower,
            jnp.concatenate([group_fresh, other_fresh], axis=1),
            jnp.concatenate([other_fresh, group_fresh], axis=1),
        )
    split_old = group_cache.reshape(cache_limit, heads_here, 2, head_dim)
    split_fresh = group_fresh.reshape(row_total, heads_here, 2, head_dim)
    attn_gates = pick_gates(group_normed, attn_router, group_routes)
    attn_tokens, attn_shares = slot_tables(
        group_routes, attn_gates, my_attn, rows_block, slot_count
    )
    token_flat = attn_tokens[:, 0, :].reshape(-1)
    share_flat = attn_shares[:, 0, :].reshape(-1)
    picked_rows = group_normed[token_flat]
    queries = jnp.einsum("sd,hdk->hsk", picked_rows, w_query, preferred_element_type=jnp.float32)
    queries = rotate(queries, (length + token_flat)[None, :]).astype(jnp.bfloat16)
    attend_heads = jax.vmap(attend, in_axes=(0, None, 1, 1, 1, 1, None))
    head_outs = attend_heads(
        queries,
        token_flat,
        split_old[:, :, 0],
        split_old[:, :, 1],
        split_fresh[:, :, 0],
        split_fresh[:, :, 1],
        length,
    )
    projected = jnp.einsum("hsk,hkd->sd", head_outs, w_out, preferred_element_type=jnp.float32)
    projected = (projected * share_flat[:, None]).reshape(block_count, slot_count, model_width)
    attn_ids = attn_tokens[:, 0, :]
    attn_own = lax.psum_scatter(
        spread_rows(projected, attn_ids, rows_block * lax.axis_size("exp")).astype(jnp.bfloat16),
        "exp",
        scatter_dimension=0,
        tiled=True,
    ).astype(jnp.float32)
    middle = lax.optimization_barrier(
        (own_rows.astype(jnp.float32) + attn_own).astype(jnp.bfloat16)
    )
    normed_mlp = rms_norm(middle, norm_mlp)
    experts_mlp = mlp_router.shape[1]
    split_count = device_count // experts_mlp
    my_expert = jnp.reshape(position // split_count, (1,))
    all_normed, all_routes = (
        lax.all_gather(normed_mlp, "exp", axis=0, tiled=True),
        lax.all_gather(mlp_routes[0], "exp", axis=0, tiled=True),
    )
    all_gates = pick_gates(all_normed, mlp_router, all_routes)
    mlp_tokens, mlp_shares = slot_tables(all_routes, all_gates, my_expert, rows_block, slot_count)
    inputs = all_normed[mlp_tokens.reshape(-1)]
    gate_part = jnp.dot(inputs, w_gate[0], preferred_element_type=jnp.float32)
    up_part = jnp.dot(inputs, w_up[0], preferred_element_type=jnp.float32)
    hidden = (jax.nn.silu(gate_part) * up_part).astype(jnp.bfloat16)
    slice_out = lax.optimization_barrier(
        jnp.dot(hidden, w_down[0], preferred_element_type=jnp.float32).astype(jnp.bfloat16)
    )
    weighted = (slice_out.astype(jnp.float32) * mlp_shares.reshape(-1)[:, None]).reshape(
        block_count, slot_count, model_width
    )
    mlp_ids = mlp_tokens[:, 0, :]
    mlp_own = lax.psum_scatter(
        spread_rows(weighted, mlp_ids, rows_block * lax.axis_size("exp")).astype(jnp.bfloat16),
        "exp",
        scatter_dimension=0,
        tiled=True,
    ).astype(jnp.float32)
    layer_out = (middle.astype(jnp.float32) + mlp_own).astype(jnp.bfloat16)
    return (layer_out[None], cache_next[None])


def solution(mesh):
    placed = (
        P("req", "exp", None),
        P("req", None, "exp"),
        P("req"),
        P("req", "exp", None),
        P("req", "exp", None),
        P(),
        P(),
        P("exp", None, None),
        P(None, "exp"),
        P("exp", None, None),
        P(),
        P(),
        P("exp", None, None),
        P("exp", None, None),
        P("exp", None, None),
    )
    return jax.shard_map(
        body,
        mesh=mesh,
        in_specs=placed,
        out_specs=(P("req", "exp", None), P("req", None, "exp")),
        check_vma=False,
    )
```

profile of v0, /device:TPU:0, one launch (start us, length us, event | category | flops | bytes accessed | tf_op | source)
XLA Modules:
  0.0 598.1 jit_solution(17848477500451785109)
XLA Ops:
  8.9 1.8 fusion.66
  11.4 2.3 copy.72
  14.5 16.4 %all-gather = s32[1,512,2]{2,0,1:T(1,128)S(1)} all-gather(s32[1,64,2]{2,0,1:T(1,128)S(1)} %copy.70), channel_id=2, replica_groups=mesh['req'=4,'exp'=8] {'exp'}, dimensions={1}, use_global_device_ids=true | all-gather | bytes 4608 | tf_op jit(solution)/shard_map/all_gather | solution.py:146
  31.8 15.1 %all-gather.1 = s32[1,512,2]{2,0,1:T(1,128)S(1)} all-gather(s32[1,64,2]{2,0,1:T(1,128)S(1)} %copy.88), channel_id=3, replica_groups=mesh['req'=4,'exp'=8] {'exp'}, dimensions={1}, use_global_device_ids=true | all-gather | bytes 4608 | tf_op jit(solution)/shard_map/all_gather | solution.py:227
  48.0 3.6 maximum_select_fusion.5
  51.6 1.8 collective-permute-start.1
  55.9 2.0 copy.73
  57.9 3.2 maximum_select_fusion.4
  61.1 38.7 %collective-permute-done.1 = bf16[1024,1024]{1,0:T(8,128)(2,1)} collective-permute-done((bf16[1024,1024]{1,0:T(8,128)(2,1)}, bf16[1024,1024]{1,0:T(8,128)(2,1)}, u32[]{:S(2)}, u32[]{:S(2)}) %collective-permute-start.1) | collective-permute-done | bytes 2097184 | tf_op jit(solution)/shard_map/ppermute | solution.py:16
  99.8 6.7 %maximum_select_fusion.2 = bf16[1024,2048]{1,0:T(8,128)(2,1)} fusion(bf16[1024,1024]{1,0:T(8,128)(2,1)} %collective-permute-done.1, bf16[1024,1024]{1,0:T(8,128)(2,1)} %maximum_select_fusion.5, pred[]{:T(512)S(6)} %eq.114), kind=kLoop, calls=%fused_computation.44 | loop fusion | flops 18874368 | bytes 8388609 | tf_op jit(solution)/shard_map/jit(_where)/select_n | solution.py:178
  106.5 2.4 collective-permute-start.2
  108.9 4.0 copy.74
  112.9 5.1 maximum_select_fusion.1
  118.0 2.9 fusion.82
  121.3 1.4 copy-done.3
  123.7 2.0 gather_fusion
  125.7 1.6 maximum_select_fusion.9
  127.3 1.8 collective-permute-start.4
  129.1 5.4 convolution_bitcast_fusion.1
  135.7 1.4 maximum_select_fusion.8
  137.1 84.4 %collective-permute-done.4 = bf16[512,1024]{0,1:T(8,128)(2,1)S(1)} collective-permute-done((bf16[512,1024]{0,1:T(8,128)(2,1)S(1)}, bf16[512,1024]{0,1:T(8,128)(2,1)S(1)}, u32[]{:S(2)}, u32[]{:S(2)}) %collective-permute-start.4) | collective-permute-done | bytes 1048608 | tf_op jit(solution)/shard_map/ppermute | solution.py:16
  221.5 2.0 maximum_select_fusion.7
  223.5 2.4 collective-permute-start.5
  225.9 1.8 maximum_select_fusion.6
  227.7 108.2 %collective-permute-done.2 = bf16[1024,2048]{1,0:T(8,128)(2,1)} collective-permute-done((bf16[1024,2048]{1,0:T(8,128)(2,1)}, bf16[1024,2048]{1,0:T(8,128)(2,1)}, u32[]{:S(2)}, u32[]{:S(2)}) %collective-permute-start.2) | collective-permute-done | bytes 4194336 | tf_op jit(solution)/shard_map/ppermute | solution.py:16
  335.9 6.4 %copy.75 = bf16[1024,2048]{0,1:T(8,128)(2,1)} copy(bf16[1024,2048]{1,0:T(8,128)(2,1)} %collective-permute-done.2) | data formatting | bytes 8388608 | tf_op jit(solution)/shard_map/ppermute | solution.py:16
  342.3 6.6 %maximum_select_fusion = bf16[1024,16,2,128]{0,3,2,1:T(8,128)(2,1)S(1)} fusion(bf16[1024,8,2,128]{0,3,2,1:T(8,128)(2,1)} %bitcast.160, bf16[1024,8,2,128]{0,3,2,1:T(8,128)(2,1)} %maximum_select_fusion.1, pred[]{:T(512)S(6)} %eq.113), kind=kLoop, calls=%fused_computation.33 | loop fusion | flops 12582912 | bytes 16777216 | tf_op jit(solution)/shard_map/jit(_where)/select_n | solution.py:178
  348.9 3.8 slice_bitcast_fusion
  352.6 1.3 broadcast_in_dim.52
  353.9 55.1 %while.16 = (s32[]{:T(128)}, f32[16,192]{1,0:T(8,128)S(1)}, f32[16,192]{1,0:T(8,128)S(1)}, f32[16,192,128]{2,1,0:T(8,128)}, s32[]{:T(128)}, /*index=5*/s32[]{:T(...) while((s32[]{:T(128)}, f32[16,192]{1,0:T(8,128)S(1)}, ...), condition=%wide.region_7.8_spmd, body=%wide.region_4.7_spmd.sunk | while | flops 823401472 | bytes 69142768 | solution.py:105
  354.7 6.4 %constant_dynamic-slice_fusion.3 = (bf16[512,16,128]{0,2,1:T(8,128)(2,1)S(1)}, bf16[512,16,128]{0,2,1:T(8,128)(2,1)}) fusion(bf16[1024,16,128]{0,2,1:T(8,128)(2,1)} %get-tuple-element.252, s32[]{:T(128)S(1)} %bitcast.175, bf16[1024,16,128]{0,2,1:T(8,128)(2,1)} %get-tuple-element.250), kind=kLoop, calls=%fused_computation.23.clone.1 | loop fusion | bytes 8388612 | tf_op jit(solution)/shard_map/vmap()/while
  361.1 3.9 copy.104
  365.0 2.7 bitcast_reduce_fusion.2
  367.7 2.6 copy-done.2
  370.4 1.8 fusion.107
  372.2 2.4 copy.105
  374.6 6.9 %multiply_add_fusion.7 = f32[16,192,128]{2,1,0:T(8,128)} fusion(f32[16,192,128]{2,1,0:T(8,128)} %get-tuple-element.233, bf16[512,16,128]{2,0,1:T(8,128)(2,1)} %copy.105, f32[16,512,192]{1,2,0:T(8,128)} %copy-done.2, f32[16,192]{1,0:T(8,128)S(1)} %max.10, pred[512]{0:T(512)(128)(4,1)S(1)} %add_compare_fusion.2, f32[16,192]{1,0:T(8,128)S(1)} %get-tuple-element.215), kind=kOutput, calls=%fused_computation.18.clone.1 | convolution fusion | flops 409731072 | bytes 11559424 | tf_op jit(solution)/shard_map/vmap()/while/body/dot_general | solution.py:86
  382.3 6.1 %constant_dynamic-slice_fusion.3 = (bf16[512,16,128]{0,2,1:T(8,128)(2,1)S(1)}, bf16[512,16,128]{0,2,1:T(8,128)(2,1)}) fusion(bf16[1024,16,128]{0,2,1:T(8,128)(2,1)} %get-tuple-element.252, s32[]{:T(128)S(1)} %bitcast.175, bf16[1024,16,128]{0,2,1:T(8,128)(2,1)} %get-tuple-element.250), kind=kLoop, calls=%fused_computation.23.clone.1 | loop fusion | bytes 8388612 | tf_op jit(solution)/shard_map/vmap()/while
  388.4 3.9 copy.104
  392.3 2.7 bitcast_reduce_fusion.2
  395.1 2.6 copy-done.2
  397.7 1.8 fusion.107
  399.5 2.4 copy.105
  402.0 6.9 %multiply_add_fusion.7 = f32[16,192,128]{2,1,0:T(8,128)} fusion(f32[16,192,128]{2,1,0:T(8,128)} %get-tuple-element.233, bf16[512,16,128]{2,0,1:T(8,128)(2,1)} %copy.105, f32[16,512,192]{1,2,0:T(8,128)} %copy-done.2, f32[16,192]{1,0:T(8,128)S(1)} %max.10, pred[512]{0:T(512)(128)(4,1)S(1)} %add_compare_fusion.2, f32[16,192]{1,0:T(8,128)S(1)} %get-tuple-element.215), kind=kOutput, calls=%fused_computation.18.clone.1 | convolution fusion | flops 409731072 | bytes 11559424 | tf_op jit(solution)/shard_map/vmap()/while/body/dot_general | solution.py:86
  409.1 4.3 maximum_select_fusion.3
  413.4 1.4 fusion.30
  415.4 2.6 copy-done.5
  418.0 2.2 fusion.31
  420.2 10.8 %fusion.39 = f32[192,2048]{1,0:T(8,128)} fusion(bf16[16,128,2048]{2,1,0:T(8,128)(2,1)} %param.26, f32[16,192,128]{2,1,0:T(8,128)S(1)} %copy-done.11, bf16[512,16,2,128]{0,3,1,2:T(8,128)(2,1)} %copy-done.8, f32[16,192,512]{2,1,0:T(8,128)} %copy-done.5, f32[16,192]{1,0:T(8,128)S(1)} %max.8, pred[192,512]{1,0:T(8,128)(4,1)S(1)} %iota_compare_fusion, ...), kind=kOutput, calls=%fused_computation.52 | convolution fusion | flops 2021523456 | bytes 20058880 | tf_op jit(solution)/shard_map/hsk,hkd->sd/dot_general | solution.py:209
  431.0 5.9 scatter_custom_fusion
  437.0 3.9 convert_element_type.190
  440.9 36.0 %reduce-scatter.3.cloned.1.call-done = bf16[64,2048]{1,0:T(8,128)(2,1)} async-done(((bf16[512,2048]{1,0:T(8,128)(2,1)}), bf16[64,2048]{1,0:T(8,128)(2,1)}) %reduce-scatter.3.cloned.1.call-update) | async-done | bytes 262160 | tf_op jit(solution)/shard_map/reduce_scatter | solution.py:212
  479.2 27.5 %all-gather.7.cloned.1.call-done = bf16[512,2048]{1,0:T(8,128)(2,1)} async-done(((bf16[64,2048]{1,0:T(8,128)(2,1)}), bf16[512,2048]{1,0:T(8,128)(2,1)}) %all-gather.7.cloned.1.call-update) | async-done | bytes 2097168 | tf_op jit(solution)/shard_map/all_gather | solution.py:226
  506.7 3.8 gather_fusion.1
  511.4 12.0 %fusion.22 = f32[192,5632]{1,0:T(8,128)} fusion(bf16[192,2048]{1,0:T(8,128)(2,1)S(1)} %gather_fusion.1, bf16[1,2048,5632]{2,1,0:T(8,128)(2,1)} %param.29), kind=kOutput, calls=%fused_computation.31 | convolution fusion | flops 4429185024 | bytes 28180480 | tf_op jit(solution)/shard_map/dot_general | solution.py:232
  523.4 20.6 %fusion.40 = bf16[192,2048]{1,0:T(8,128)(2,1)S(1)} fusion(bf16[1,5632,2048]{2,1,0:T(8,128)(2,1)} %param.31, bf16[192,2048]{1,0:T(8,128)(2,1)} %copy-done.12, bf16[1,2048,5632]{2,1,0:T(8,128)(2,1)} %param.30, f32[192,5632]{1,0:T(8,128)} %fusion.22), kind=kOutput, calls=%fused_computation.53 | convolution fusion | flops 8865251328 | bytes 52035584 | tf_op jit(solution)/shard_map/dot_general | solution.py:236
  545.1 5.2 scatter_custom_fusion.1
  550.3 3.8 convert_element_type.202
  554.2 2.2 copy.90
  556.4 1.2 broadcast_in_dim.60
  557.6 4.1 dynamic_update_slice.3
  561.8 3.0 select_bitcast_fusion
  564.8 24.8 %reduce-scatter.5.cloned.1.call-done = bf16[64,2048]{1,0:T(8,128)(2,1)} async-done(((bf16[512,2048]{1,0:T(8,128)(2,1)}), bf16[64,2048]{1,0:T(8,128)(2,1)}) %reduce-scatter.5.cloned.1.call-update) | async-done | bytes 262160 | tf_op jit(solution)/shard_map/reduce_scatter | solution.py:242
  589.6 1.7 fusion.68
  (138 shorter events, 15.9 us)
Async XLA Ops:
  7.2 110.8 %copy-start = (bf16[2048,512]{1,0:T(8,128)(2,1)S(1)}, bf16[2048,512]{1,0:T(8,128)(2,1)}, u32[]{:S(2)}) copy-start(bf16[2048,512]{1,0:T(8,128)(2,1)} %param.25) | copy-start | bytes 6291460
  7.2 40.8 %copy-start.6 = (bf16[1,1024,512]{2,1,0:T(8,128)(2,1)S(1)}, bf16[1,1024,512]{2,1,0:T(8,128)(2,1)}, u32[]{:S(2)}) copy-start(bf16[1,1024,512]{2,1,0:T(8,128)(2,1)} %param.18) | copy-start | bytes 3145732
  7.2 110.8 %all-gather.5.cloned.1.call-start = ((), (), s32[]{:S(2)}) async-start(), calls=%async_computation.2 | async-start | bytes 2359296 | tf_op jit(solution)/shard_map/all_gather | solution.py:145
  7.2 40.8 %collective-permute-start = (bf16[1024,512]{1,0:T(8,128)(2,1)}, bf16[1024,512]{1,0:T(8,128)(2,1)}, u32[]{:S(2)}, u32[]{:S(2)}) collective-permute-start(bf16[1024,512]{1,0:T(8,128)(2,1)} %bitcast.161), channel_id=1, source_target_pairs={{0,1},{1,0},{2,3},{3,2},{4,5},{5,4},{6,7},{7,6},{8,9},{9,8},{10,11... | collective-permute-start | bytes 3145736 | tf_op jit(solution)/shard_map/ppermute | solution.py:16
  10.7 466.2 %reduce-scatter.3.cloned.1.call-start = ((), (), s32[]{:S(2)}) async-start(), calls=%async_computation.3 | async-start | bytes 2359296 | tf_op jit(solution)/shard_map/reduce_scatter | solution.py:212
  46.9 7.0 %copy-start.15 = (s32[1,512,2]{1,2,0:T(2,128)}, s32[1,512,2]{1,2,0:T(2,128)S(1)}, u32[]{:S(2)}) copy-start(s32[1,512,2]{1,2,0:T(2,128)S(1)} %copy.89) | copy-start | bytes 12292
  48.0 6.0 copy-start.21
  51.6 48.2 %collective-permute-start.1 = (bf16[1024,1024]{1,0:T(8,128)(2,1)}, bf16[1024,1024]{1,0:T(8,128)(2,1)}, u32[]{:S(2)}, u32[]{:S(2)}) collective-permute-start(bf16[1024,1024]{1,0:T(8,128)(2,1)} %maximum_select_fusion.5), channel_id=1, source_target_pairs={{0,2},{1,3},{2,0},{3,1},{4,6},{5,7},{6,4},{7,5},{8,10},{9,11},{10,... | collective-permute-start | bytes 6291464 | tf_op jit(solution)/shard_map/ppermute | solution.py:16
  53.6 0.6 copy-start.17
  106.5 229.4 %collective-permute-start.2 = (bf16[1024,2048]{1,0:T(8,128)(2,1)}, bf16[1024,2048]{1,0:T(8,128)(2,1)}, u32[]{:S(2)}, u32[]{:S(2)}) collective-permute-start(bf16[1024,2048]{1,0:T(8,128)(2,1)} %maximum_select_fusion.2), channel_id=1, source_target_pairs={{0,4},{1,5},{2,6},{3,7},{4,0},{5,1},{6,2},{7,3},{8,12},{9,13},{10,... | collective-permute-start | bytes 12582920 | tf_op jit(solution)/shard_map/ppermute | solution.py:16
  120.9 1.8 copy-start.3
  120.9 1.8 copy-start.19
  121.2 4.5 copy-start.9
  121.2 4.5 collective-permute-start.3
  127.3 7.3 %copy-start.13 = (f32[192,64]{1,0:T(8,128)S(1)}, f32[192,64]{1,0:T(8,128)}, u32[]{:S(2)}) copy-start(f32[192,64]{1,0:T(8,128)} %get-tuple-element.140) | copy-start | bytes 147460
  127.3 7.3 %copy-start.14 = (f32[192,64]{1,0:T(8,128)S(1)}, f32[192,64]{1,0:T(8,128)}, u32[]{:S(2)}) copy-start(f32[192,64]{1,0:T(8,128)} %get-tuple-element.141) | copy-start | bytes 147460
  127.3 94.2 %collective-permute-start.4 = (bf16[512,1024]{0,1:T(8,128)(2,1)S(1)}, bf16[512,1024]{0,1:T(8,128)(2,1)S(1)}, u32[]{:S(2)}, u32[]{:S(2)}) collective-permute-start(bf16[512,1024]{0,1:T(8,128)(2,1)S(1)} %maximum_select_fusion.9), channel_id=1, source_target_pairs={{0,2},{1,3},{2,0},{3,1},{4,6},{5,7},{6,4},{7,5},{8,10},{9,11},{10,... | collective-permute-start | bytes 3145736 | tf_op jit(solution)/shard_map/ppermute | solution.py:16
  223.5 185.5 %collective-permute-start.5 = (bf16[512,2048]{0,1:T(8,128)(2,1)}, bf16[512,2048]{0,1:T(8,128)(2,1)}, u32[]{:S(2)}, u32[]{:S(2)}) collective-permute-start(bf16[512,2048]{0,1:T(8,128)(2,1)} %maximum_select_fusion.7), channel_id=1, source_target_pairs={{0,4},{1,5},{2,6},{3,7},{4,0},{5,1},{6,2},{7,3},{8,12},{9,13},{10,... | collective-permute-start | bytes 6291464 | tf_op jit(solution)/shard_map/ppermute | solution.py:16
  367.7 2.7 copy-start.2
  395.0 2.7 copy-start.2
  413.3 2.0 copy-start.8
  415.4 2.7 copy-start.5
  415.4 4.9 copy-start.11
  437.0 40.0 %copy-start.10 = (bf16[1,64,2048]{2,1,0:T(8,128)(2,1)S(1)}, bf16[1,64,2048]{2,1,0:T(8,128)(2,1)}, u32[]{:S(2)}) copy-start(bf16[1,64,2048]{2,1,0:T(8,128)(2,1)} %param.17) | copy-start | bytes 786436
  437.0 41.1 %copy-start.23 = (f32[2048]{0:T(1024)S(1)}, f32[2048]{0:T(1024)}, u32[]{:S(2)}) copy-start(f32[2048]{0:T(1024)} %param.27) | copy-start | bytes 24580
  440.9 65.9 %all-gather.7.cloned.1.call-start = ((), (), s32[]{:S(2)}) async-start(), calls=%async_computation.4 | async-start | bytes 2359296 | tf_op jit(solution)/shard_map/all_gather | solution.py:226
  479.0 110.6 %reduce-scatter.5.cloned.1.call-start = ((), (), s32[]{:S(2)}) async-start(), calls=%async_computation.5 | async-start | bytes 2359296 | tf_op jit(solution)/shard_map/reduce_scatter | solution.py:242
  510.5 0.9 copy-start.12
  523.3 20.7 %copy-start.4 = (bf16[512,2048]{1,0:T(8,128)(2,1)S(1)}, bf16[512,2048]{1,0:T(8,128)(2,1)}, u32[]{:S(2)}) copy-start(bf16[512,2048]{1,0:T(8,128)(2,1)} %all-gather.7.cloned.1.call-done) | copy-start | bytes 6291460
  523.3 20.7 %copy-start.20 = (bf16[2048,8]{0,1:T(8,128)(2,1)S(1)}, bf16[2048,8]{0,1:T(8,128)(2,1)}, u32[]{:S(2)}) copy-start(bf16[2048,8]{0,1:T(8,128)(2,1)} %param.28) | copy-start | bytes 98308
  523.4 21.3 %copy-start.16 = (s32[1,512,2]{1,2,0:T(2,128)S(1)}, s32[1,512,2]{1,2,0:T(2,128)}, u32[]{:S(2)}) copy-start(s32[1,512,2]{1,2,0:T(2,128)} %copy-done.15) | copy-start | bytes 12292
  523.4 21.5 %copy-start.18 = (s32[8,64]{1,0:T(8,128)S(1)}, s32[8,64]{1,0:T(8,128)}, u32[]{:S(2)}) copy-start(s32[8,64]{1,0:T(8,128)} %copy-done.17) | copy-start | bytes 6148
  523.4 21.5 %copy-start.22 = (pred[8,64]{1,0:T(8,128)(4,1)S(1)}, pred[8,64]{1,0:T(8,128)(4,1)}, u32[]{:S(2)}) copy-start(pred[8,64]{1,0:T(8,128)(4,1)} %copy-done.21) | copy-start | bytes 1540
  554.1 7.6 %copy-start.7 = (bf16[1,1024,512]{2,1,0:T(8,128)(2,1)S(1)}, bf16[1,1024,512]{2,1,0:T(8,128)(2,1)}, u32[]{:S(2)}) copy-start(bf16[1,1024,512]{2,1,0:T(8,128)(2,1)} %param.18) | copy-start | bytes 3145732
  554.2 37.1 %copy-start.1 = (bf16[2048,512]{1,0:T(8,128)(2,1)S(1)}, bf16[2048,512]{1,0:T(8,128)(2,1)}, u32[]{:S(2)}) copy-start(bf16[2048,512]{1,0:T(8,128)(2,1)} %param.25) | copy-start | bytes 6291460
Sparse Core Ops, SparseCore 0:
  10.8 34.0 all-gather.4
  441.0 35.8 reduce-scatter.2
  479.1 27.5 all-gather.6
  554.3 35.2 reduce-scatter.4
where the time goes:
time: 603 us; the launch traced here: 598 us
  waiting for transfers between devices  320 us (53%)
  other arithmetic  76.5 us (13%)
  matrix products  73.7 us (12%)
  local copies, waits for them, and re-layouts  72 us (12%)
  blocking collectives  31.5 us (5%)
  between operations  15.2 us (3%)
  starting transfers between devices  9.33 us (2%)
    ppermute x6, waiting for transfers between devices, from_partner(): return lax.ppermute(value, axis, pairs)  231 us
    reduce_scatter x1, waiting for transfers between devices, body(): lax.psum_scatter(spread_rows(projected, attn_ids, rows_block * lax.axis_s...  36 us
    while x12, local copies, waits for them, and re-layouts  30.4 us
    all_gather x1, waiting for transfers between devices, body(): lax.all_gather(normed_mlp, 'exp', axis=0, tiled=True)  27.5 us
    select_n x5, other arithmetic, body(): jnp.where(lower, jnp.concatenate([group_cache, other_cache], axis=1), jnp...  25.2 us
    reduce_scatter x1, waiting for transfers between devices, body(): lax.psum_scatter(spread_rows(weighted, mlp_ids, rows_block * lax.axis_siz...  24.8 us
    dot_general x1, matrix products, body(): jnp.dot(hidden, w_down[0], preferred_element_type=jnp.float32)  20.6 us
    all_gather x1, blocking collectives, body(): lax.all_gather(attn_routes[0], 'exp', axis=0, tiled=True)  16.4 us
  transfers between devices with their start and end apart: 10, of which 6 were waited for; matrix products, arithmetic and copies ran while one was open for 22% of the time, Pallas kernels for 0%

commit v1 on v0

--- a/solution.py
+++ b/solution.py
@@ -8,6 +8,14 @@
 epsilon = 1e-05
 rope_base = 10000.0
 masked_score = -1e30
+
+
+def begin_cubes_in(patch, axis_no):
+    patch = jnp.moveaxis(patch, 0, axis_no)
+    latest = patch.shape
+    return patch.reshape(
+        *latest[:axis_no], latest[axis_no] * latest[axis_no + 1], *latest[axis_no + 2 :]
+    )
 
 
 def from_partner(value, axis, stride):
@@ -222,8 +230,30 @@
     experts_mlp = mlp_router.shape[1]
     split_count = device_count // experts_mlp
     my_expert = jnp.reshape(position // split_count, (1,))
+
+    def _match_flows(named_axis, frame, dim_no):
+        full_n = lax.axis_size(named_axis)
+        block_last = range(full_n)
+        small = map(lambda p: (p, (p + 1) % full_n), block_last)
+        entries = list(small)
+        series = [(q, at) for at, q in entries]
+        arr_now, local_out = ([], [])
+        for d in tuple(range(full_n - 1)):
+            if d % 2 == 0:
+                block_next = lax.ppermute(arr_now[-1] if arr_now else frame, named_axis, entries)
+                arr_now.append(block_next)
+            else:
+                frame_out = lax.ppermute(local_out[-1] if local_out else frame, named_axis, series)
+                local_out.append(frame_out)
+        val2 = jnp.stack([*arr_now[::-1], frame, *local_out])
+        mid_arr = lax.axis_index(named_axis)
+        taken_in = len(arr_now)
+        later = mid_arr - taken_in
+        val2 = val2[(jnp.arange(full_n) - later) % full_n]
+        return begin_cubes_in(val2, dim_no)
+
     all_normed, all_routes = (
-        lax.all_gather(normed_mlp, "exp", axis=0, tiled=True),
+        _match_flows("exp", normed_mlp, 0),
         lax.all_gather(mlp_routes[0], "exp", axis=0, tiled=True),
     )
     all_gates = pick_gates(all_normed, mlp_router, all_routes)

time: 603 us -> 602 us (level)
  starting transfers between devices: 9.33 us -> 20.3 us
  waiting for transfers between devices: 320 us -> 310 us
    all_gather x1 -> x0, waiting for transfers between devices: 27.5 us -> none  [body(): lax.all_gather(normed_mlp, 'exp', axis=0, tiled=True)]
    ppermute x0 -> x7, waiting for transfers between devices: none -> 19.7 us  [the longest x4 19.5 us: _match_flows(): lax.ppermute(arr_now[-1] if arr_now else frame, named_axis, entries)]
    ppermute x0 -> x7, starting transfers between devices: none -> 11.2 us  [the longest x3 11.2 us: _match_flows(): lax.ppermute(local_out[-1] if local_out else frame, named_axis, series)]
  transfers between devices with their start and end apart: 10 -> 16, of which waited for: 6 -> 10; matrix products, arithmetic and copies ran while one was open for 22% -> 23% of each run, Pallas kernels for 0% -> 0%
where the time goes in v1:
time: 602 us; the launch traced here: 597 us
  waiting for transfers between devices  310 us (51%)
  other arithmetic  76.9 us (13%)
  matrix products  73.4 us (12%)
  local copies, waits for them, and re-layouts  70.2 us (12%)
  blocking collectives  31.3 us (5%)
  starting transfers between devices  20.3 us (3%)
  between operations  15.2 us (3%)
    ppermute x6, waiting for transfers between devices, from_partner(): return lax.ppermute(value, axis, pairs)  231 us
    reduce_scatter x1, waiting for transfers between devices, body(): lax.psum_scatter(spread_rows(projected, attn_ids, rows_block * lax.axis_s...  35.9 us
    while x12, local copies, waits for them, and re-layouts  26.8 us
    select_n x5, other arithmetic, body(): jnp.where(lower, jnp.concatenate([group_cache, other_cache], axis=1), jnp...  25.2 us
    reduce_scatter x1, waiting for transfers between devices, body(): lax.psum_scatter(spread_rows(weighted, mlp_ids, rows_block * lax.axis_siz...  23.6 us
    dot_general x1, matrix products, body(): jnp.dot(hidden, w_down[0], preferred_element_type=jnp.float32)  20.5 us
    ppermute x4, waiting for transfers between devices, _match_flows(): lax.ppermute(arr_now[-1] if arr_now else frame, named_axis, entries)  19.5 us
    all_gather x1, blocking collectives, body(): lax.all_gather(attn_routes[0], 'exp', axis=0, tiled=True)  16.2 us
  transfers between devices with their start and end apart: 16, of which 10 were waited for; matrix products, arithmetic and copies ran while one was open for 23% of the time, Pallas kernels for 0%

profile of v1, /device:TPU:0, one launch (start us, length us, event | category | flops | bytes accessed | tf_op | source)
XLA Modules:
  0.0 597.5 jit_solution(13725021784859299663)
XLA Ops:
  9.0 1.9 fusion.66
  11.6 2.3 copy.72
  14.0 16.2 %all-gather = s32[1,512,2]{2,0,1:T(1,128)S(1)} all-gather(s32[1,64,2]{2,0,1:T(1,128)S(1)} %copy.70), channel_id=2, replica_groups=mesh['req'=4,'exp'=8] {'exp'}, dimensions={1}, use_global_device_ids=true | all-gather | bytes 4608 | tf_op jit(solution)/shard_map/all_gather | solution.py:154
  30.4 15.1 %all-gather.1 = s32[1,512,2]{2,0,1:T(1,128)S(1)} all-gather(s32[1,64,2]{2,0,1:T(1,128)S(1)} %copy.88), channel_id=3, replica_groups=mesh['req'=4,'exp'=8] {'exp'}, dimensions={1}, use_global_device_ids=true | all-gather | bytes 4608 | tf_op jit(solution)/shard_map/all_gather | solution.py:257
  46.7 3.6 maximum_select_fusion.5
  50.2 1.7 collective-permute-start.1
  54.4 2.7 copy.73
  57.2 3.2 maximum_select_fusion.4
  60.4 38.0 %collective-permute-done.1 = bf16[1024,1024]{1,0:T(8,128)(2,1)} collective-permute-done((bf16[1024,1024]{1,0:T(8,128)(2,1)}, bf16[1024,1024]{1,0:T(8,128)(2,1)}, u32[]{:S(2)}, u32[]{:S(2)}) %collective-permute-start.1) | collective-permute-done | bytes 2097184 | tf_op jit(solution)/shard_map/ppermute | solution.py:24
  98.4 6.7 %maximum_select_fusion.2 = bf16[1024,2048]{1,0:T(8,128)(2,1)} fusion(bf16[1024,1024]{1,0:T(8,128)(2,1)} %collective-permute-done.1, bf16[1024,1024]{1,0:T(8,128)(2,1)} %maximum_select_fusion.5, pred[]{:T(512)S(6)} %eq.116), kind=kLoop, calls=%fused_computation.45 | loop fusion | flops 18874368 | bytes 8388609 | tf_op jit(solution)/shard_map/jit(_where)/select_n | solution.py:186
  105.2 2.4 collective-permute-start.2
  107.5 4.0 copy.74
  111.5 5.1 maximum_select_fusion.1
  116.6 2.9 fusion.84
  119.9 1.4 copy-done.3
  122.3 2.0 gather_fusion
  124.4 1.7 maximum_select_fusion.9
  126.1 1.8 collective-permute-start.4
  127.9 5.2 convolution_bitcast_fusion.1
  134.2 1.4 maximum_select_fusion.8
  135.6 84.5 %collective-permute-done.4 = bf16[512,1024]{0,1:T(8,128)(2,1)S(1)} collective-permute-done((bf16[512,1024]{0,1:T(8,128)(2,1)S(1)}, bf16[512,1024]{0,1:T(8,128)(2,1)S(1)}, u32[]{:S(2)}, u32[]{:S(2)}) %collective-permute-start.4) | collective-permute-done | bytes 1048608 | tf_op jit(solution)/shard_map/ppermute | solution.py:24
  220.1 2.0 maximum_select_fusion.7
  222.2 2.4 collective-permute-start.5
  224.6 1.8 maximum_select_fusion.6
  226.3 108.2 %collective-permute-done.2 = bf16[1024,2048]{1,0:T(8,128)(2,1)} collective-permute-done((bf16[1024,2048]{1,0:T(8,128)(2,1)}, bf16[1024,2048]{1,0:T(8,128)(2,1)}, u32[]{:S(2)}, u32[]{:S(2)}) %collective-permute-start.2) | collective-permute-done | bytes 4194336 | tf_op jit(solution)/shard_map/ppermute | solution.py:24
  334.5 6.4 %copy.75 = bf16[1024,2048]{0,1:T(8,128)(2,1)} copy(bf16[1024,2048]{1,0:T(8,128)(2,1)} %collective-permute-done.2) | data formatting | bytes 8388608 | tf_op jit(solution)/shard_map/ppermute | solution.py:24
  340.9 6.6 %maximum_select_fusion = bf16[1024,16,2,128]{0,3,2,1:T(8,128)(2,1)S(1)} fusion(bf16[1024,8,2,128]{0,3,2,1:T(8,128)(2,1)} %bitcast.181, bf16[1024,8,2,128]{0,3,2,1:T(8,128)(2,1)} %maximum_select_fusion.1, pred[]{:T(512)S(6)} %eq.115), kind=kLoop, calls=%fused_computation.34 | loop fusion | flops 12582912 | bytes 16777216 | tf_op jit(solution)/shard_map/jit(_where)/select_n | solution.py:186
  347.5 3.8 slice_bitcast_fusion
  352.6 51.5 %while.16 = (s32[]{:T(128)}, f32[16,192]{1,0:T(8,128)S(1)}, f32[16,192]{1,0:T(8,128)S(1)}, f32[16,192,128]{2,1,0:T(8,128)}, s32[]{:T(128)}, /*index=5*/s32[]{:T(...) while((s32[]{:T(128)}, f32[16,192]{1,0:T(8,128)S(1)}, ...), condition=%wide.region_7.8_spmd, body=%wide.region_4.7_spmd.sunk | while | flops 823401472 | bytes 69142768 | solution.py:113
  353.3 6.4 %constant_dynamic-slice_fusion.3 = (bf16[512,16,128]{0,2,1:T(8,128)(2,1)S(1)}, bf16[512,16,128]{0,2,1:T(8,128)(2,1)}) fusion(bf16[1024,16,128]{0,2,1:T(8,128)(2,1)} %get-tuple-element.252, s32[]{:T(128)S(1)} %bitcast.196, bf16[1024,16,128]{0,2,1:T(8,128)(2,1)} %get-tuple-element.250), kind=kLoop, calls=%fused_computation.24.clone.1 | loop fusion | bytes 8388612 | tf_op jit(solution)/shard_map/vmap()/while
  359.7 3.9 copy.104
  363.6 2.7 bitcast_reduce_fusion.2
  366.4 1.8 fusion.109
  369.0 2.4 copy.105
  371.4 6.9 %multiply_add_fusion.7 = f32[16,192,128]{2,1,0:T(8,128)} fusion(f32[16,192,128]{2,1,0:T(8,128)} %get-tuple-element.233, bf16[512,16,128]{2,0,1:T(8,128)(2,1)} %copy.105, f32[16,512,192]{1,2,0:T(8,128)} %copy-done.2, f32[16,192]{1,0:T(8,128)S(1)} %max.10, pred[512]{0:T(512)(128)(4,1)S(1)} %add_compare_fusion.2, f32[16,192]{1,0:T(8,128)S(1)} %get-tuple-element.215), kind=kOutput, calls=%fused_computation.19.clone.1 | convolution fusion | flops 409731072 | bytes 11559424 | tf_op jit(solution)/shard_map/vmap()/while/body/dot_general | solution.py:94
  379.1 6.1 %constant_dynamic-slice_fusion.3 = (bf16[512,16,128]{0,2,1:T(8,128)(2,1)S(1)}, bf16[512,16,128]{0,2,1:T(8,128)(2,1)}) fusion(bf16[1024,16,128]{0,2,1:T(8,128)(2,1)} %get-tuple-element.252, s32[]{:T(128)S(1)} %bitcast.196, bf16[1024,16,128]{0,2,1:T(8,128)(2,1)} %get-tuple-element.250), kind=kLoop, calls=%fused_computation.24.clone.1 | loop fusion | bytes 8388612 | tf_op jit(solution)/shard_map/vmap()/while
  385.2 3.9 copy.104
  389.1 2.7 bitcast_reduce_fusion.2
  391.9 1.8 fusion.109
  394.5 2.4 copy.105
  396.9 6.9 %multiply_add_fusion.7 = f32[16,192,128]{2,1,0:T(8,128)} fusion(f32[16,192,128]{2,1,0:T(8,128)} %get-tuple-element.233, bf16[512,16,128]{2,0,1:T(8,128)(2,1)} %copy.105, f32[16,512,192]{1,2,0:T(8,128)} %copy-done.2, f32[16,192]{1,0:T(8,128)S(1)} %max.10, pred[512]{0:T(512)(128)(4,1)S(1)} %add_compare_fusion.2, f32[16,192]{1,0:T(8,128)S(1)} %get-tuple-element.215), kind=kOutput, calls=%fused_computation.19.clone.1 | convolution fusion | flops 409731072 | bytes 11559424 | tf_op jit(solution)/shard_map/vmap()/while/body/dot_general | solution.py:94
  404.1 4.3 maximum_select_fusion.3
  408.3 1.4 fusion.30
  410.4 2.2 fusion.31
  413.1 10.8 %fusion.39 = f32[192,2048]{1,0:T(8,128)} fusion(bf16[16,128,2048]{2,1,0:T(8,128)(2,1)} %param.26, f32[16,192,128]{2,1,0:T(8,128)S(1)} %copy-done.12, bf16[512,16,2,128]{0,3,1,2:T(8,128)(2,1)} %copy-done.7, f32[16,192,512]{2,1,0:T(8,128)} %copy-done.4, f32[16,192]{1,0:T(8,128)S(1)} %max.8, pred[192,512]{1,0:T(8,128)(4,1)S(1)} %iota_compare_fusion, ...), kind=kOutput, calls=%fused_computation.53 | convolution fusion | flops 2021523456 | bytes 20058880 | tf_op jit(solution)/shard_map/hsk,hkd->sd/dot_general | solution.py:217
  423.8 5.9 scatter_custom_fusion
  429.8 3.8 convert_element_type.190
  433.7 35.9 %reduce-scatter.3.cloned.1.call-done = bf16[64,2048]{1,0:T(8,128)(2,1)} async-done(((bf16[512,2048]{1,0:T(8,128)(2,1)}), bf16[64,2048]{1,0:T(8,128)(2,1)}) %reduce-scatter.3.cloned.1.call-update) | async-done | bytes 262160 | tf_op jit(solution)/shard_map/reduce_scatter | solution.py:220
  471.0 7.8 %collective-permute-done.6 = bf16[64,2048]{1,0:T(8,128)(2,1)S(1)} collective-permute-done((bf16[64,2048]{1,0:T(8,128)(2,1)S(1)}, bf16[64,2048]{1,0:T(8,128)(2,1)S(1)}, u32[]{:S(2)}, u32[]{:S(2)}) %collective-permute-start.6) | collective-permute-done | bytes 262176 | tf_op jit(solution)/shard_map/ppermute | solution.py:243
  478.8 3.5 collective-permute-start.10
  482.3 4.2 collective-permute-done.7
  486.6 3.8 collective-permute-start.11
  490.4 3.9 collective-permute-done.8
  494.3 3.8 collective-permute-start.12
  498.2 3.7 collective-permute-done.9
  507.8 2.3 gather_fusion.1
  512.1 12.0 %fusion.22 = f32[192,5632]{1,0:T(8,128)} fusion(bf16[192,2048]{1,0:T(8,128)(2,1)S(1)} %gather_fusion.2, bf16[1,2048,5632]{2,1,0:T(8,128)(2,1)} %param.29), kind=kOutput, calls=%fused_computation.32 | convolution fusion | flops 4429185024 | bytes 28180480 | tf_op jit(solution)/shard_map/dot_general | solution.py:262
  524.1 20.5 %fusion.40 = bf16[192,2048]{1,0:T(8,128)(2,1)S(1)} fusion(bf16[1,5632,2048]{2,1,0:T(8,128)(2,1)} %param.31, bf16[192,2048]{1,0:T(8,128)(2,1)} %copy-done.14, bf16[1,2048,5632]{2,1,0:T(8,128)(2,1)} %param.30, f32[192,5632]{1,0:T(8,128)} %fusion.22), kind=kOutput, calls=%fused_computation.54 | convolution fusion | flops 8865251328 | bytes 52035584 | tf_op jit(solution)/shard_map/dot_general | solution.py:266
  545.7 5.2 scatter_custom_fusion.1
  550.9 3.8 convert_element_type.202
  558.0 4.3 dynamic_update_slice.3
  562.3 3.0 select_bitcast_fusion
  565.4 23.6 %reduce-scatter.5.cloned.1.call-done = bf16[64,2048]{1,0:T(8,128)(2,1)} async-done(((bf16[512,2048]{1,0:T(8,128)(2,1)}), bf16[64,2048]{1,0:T(8,128)(2,1)}) %reduce-scatter.5.cloned.1.call-update) | async-done | bytes 262160 | tf_op jit(solution)/shard_map/reduce_scatter | solution.py:272
  589.0 1.7 fusion.68
  (168 shorter events, 27.4 us)
Async XLA Ops:
  7.2 109.4 %copy-start = (bf16[2048,512]{1,0:T(8,128)(2,1)S(1)}, bf16[2048,512]{1,0:T(8,128)(2,1)}, u32[]{:S(2)}) copy-start(bf16[2048,512]{1,0:T(8,128)(2,1)} %param.25) | copy-start | bytes 6291460
  7.2 6.7 %copy-start.26 = (s32[1,64,2]{1,2,0:T(2,128)S(1)}, s32[1,64,2]{1,2,0:T(2,128)}, u32[]{:S(2)}) copy-start(s32[1,64,2]{1,2,0:T(2,128)} %param.20) | copy-start | bytes 1540
  7.2 23.1 %copy-start.27 = (s32[1,64,2]{1,2,0:T(2,128)S(1)}, s32[1,64,2]{1,2,0:T(2,128)}, u32[]{:S(2)}) copy-start(s32[1,64,2]{1,2,0:T(2,128)} %param.21) | copy-start | bytes 1540
  7.2 109.4 %all-gather.4.cloned.1.call-start = ((), (), s32[]{:S(2)}) async-start(), calls=%async_computation.2 | async-start | bytes 2359296 | tf_op jit(solution)/shard_map/all_gather | solution.py:153
  7.2 39.4 %collective-permute-start = (bf16[1024,512]{1,0:T(8,128)(2,1)}, bf16[1024,512]{1,0:T(8,128)(2,1)}, u32[]{:S(2)}, u32[]{:S(2)}) collective-permute-start(bf16[1024,512]{1,0:T(8,128)(2,1)} %bitcast.182), channel_id=1, source_target_pairs={{0,1},{1,0},{2,3},{3,2},{4,5},{5,4},{6,7},{7,6},{8,9},{9,8},{10,11... | collective-permute-start | bytes 3145736 | tf_op jit(solution)/shard_map/ppermute | solution.py:24
  8.9 37.7 %copy-start.5 = (bf16[1,1024,512]{2,1,0:T(8,128)(2,1)S(1)}, bf16[1,1024,512]{2,1,0:T(8,128)(2,1)}, u32[]{:S(2)}) copy-start(bf16[1,1024,512]{2,1,0:T(8,128)(2,1)} %param.18) | copy-start | bytes 3145732
  10.9 458.8 %reduce-scatter.3.cloned.1.call-start = ((), (), s32[]{:S(2)}) async-start(), calls=%async_computation.3 | async-start | bytes 2359296 | tf_op jit(solution)/shard_map/reduce_scatter | solution.py:220
  45.6 4.6 copy-start.17
  46.6 5.6 copy-start.24
  50.2 7.0 %copy-start.10 = (bf16[1,1024,512]{1,2,0:T(8,128)(2,1)S(1)}, bf16[1,1024,512]{1,2,0:T(8,128)(2,1)}, u32[]{:S(2)}) copy-start(bf16[1,1024,512]{1,2,0:T(8,128)(2,1)} %copy.72) | copy-start | bytes 3145732
  50.2 48.2 %collective-permute-start.1 = (bf16[1024,1024]{1,0:T(8,128)(2,1)}, bf16[1024,1024]{1,0:T(8,128)(2,1)}, u32[]{:S(2)}, u32[]{:S(2)}) collective-permute-start(bf16[1024,1024]{1,0:T(8,128)(2,1)} %maximum_select_fusion.5), channel_id=1, source_target_pairs={{0,2},{1,3},{2,0},{3,1},{4,6},{5,7},{6,4},{7,5},{8,10},{9,11},{10,... | collective-permute-start | bytes 6291464 | tf_op jit(solution)/shard_map/ppermute | solution.py:24
  52.2 0.6 copy-start.19
  105.2 229.4 %collective-permute-start.2 = (bf16[1024,2048]{1,0:T(8,128)(2,1)}, bf16[1024,2048]{1,0:T(8,128)(2,1)}, u32[]{:S(2)}, u32[]{:S(2)}) collective-permute-start(bf16[1024,2048]{1,0:T(8,128)(2,1)} %maximum_select_fusion.2), channel_id=1, source_target_pairs={{0,4},{1,5},{2,6},{3,7},{4,0},{5,1},{6,2},{7,3},{8,12},{9,13},{10,... | collective-permute-start | bytes 12582920 | tf_op jit(solution)/shard_map/ppermute | solution.py:24
  119.5 1.8 copy-start.3
  119.5 1.8 copy-start.21
  119.8 4.6 copy-start.8
  119.8 4.6 collective-permute-start.3
  124.4 3.5 copy-start.13
  126.1 7.0 %copy-start.15 = (f32[192,64]{1,0:T(8,128)S(1)}, f32[192,64]{1,0:T(8,128)}, u32[]{:S(2)}) copy-start(f32[192,64]{1,0:T(8,128)} %get-tuple-element.140) | copy-start | bytes 147460
  126.1 7.0 %copy-start.16 = (f32[192,64]{1,0:T(8,128)S(1)}, f32[192,64]{1,0:T(8,128)}, u32[]{:S(2)}) copy-start(f32[192,64]{1,0:T(8,128)} %get-tuple-element.141) | copy-start | bytes 147460
  126.1 94.1 %collective-permute-start.4 = (bf16[512,1024]{0,1:T(8,128)(2,1)S(1)}, bf16[512,1024]{0,1:T(8,128)(2,1)S(1)}, u32[]{:S(2)}, u32[]{:S(2)}) collective-permute-start(bf16[512,1024]{0,1:T(8,128)(2,1)S(1)} %maximum_select_fusion.9), channel_id=1, source_target_pairs={{0,2},{1,3},{2,0},{3,1},{4,6},{5,7},{6,4},{7,5},{8,10},{9,11},{10,... | collective-permute-start | bytes 3145736 | tf_op jit(solution)/shard_map/ppermute | solution.py:24
  222.2 181.9 %collective-permute-start.5 = (bf16[512,2048]{0,1:T(8,128)(2,1)}, bf16[512,2048]{0,1:T(8,128)(2,1)}, u32[]{:S(2)}, u32[]{:S(2)}) collective-permute-start(bf16[512,2048]{0,1:T(8,128)(2,1)} %maximum_select_fusion.7), channel_id=1, source_target_pairs={{0,4},{1,5},{2,6},{3,7},{4,0},{5,1},{6,2},{7,3},{8,12},{9,13},{10,... | collective-permute-start | bytes 6291464 | tf_op jit(solution)/shard_map/ppermute | solution.py:24
  366.3 2.7 copy-start.2
  391.8 2.7 copy-start.2
  408.3 2.0 copy-start.7
  410.4 2.7 copy-start.4
  410.4 2.7 copy-start.12
  433.6 36.0 %copy-start.11 = (bf16[1,64,2048]{2,1,0:T(8,128)(2,1)S(1)}, bf16[1,64,2048]{2,1,0:T(8,128)(2,1)}, u32[]{:S(2)}) copy-start(bf16[1,64,2048]{2,1,0:T(8,128)(2,1)} %param.17) | copy-start | bytes 786436
  433.6 37.2 %copy-start.23 = (f32[2048]{0:T(1024)S(1)}, f32[2048]{0:T(1024)}, u32[]{:S(2)}) copy-start(f32[2048]{0:T(1024)} %param.27) | copy-start | bytes 24580
  433.6 155.3 %reduce-scatter.5.cloned.1.call-start = ((), (), s32[]{:S(2)}) async-start(), calls=%async_computation.4 | async-start | bytes 2359296 | tf_op jit(solution)/shard_map/reduce_scatter | solution.py:272
  470.9 7.8 %collective-permute-start.6 = (bf16[64,2048]{1,0:T(8,128)(2,1)S(1)}, bf16[64,2048]{1,0:T(8,128)(2,1)S(1)}, u32[]{:S(2)}, u32[]{:S(2)}) collective-permute-start(bf16[64,2048]{1,0:T(8,128)(2,1)S(1)} %fusion.62), channel_id=1, source_target_pairs={{0,1},{1,2},{2,3},{3,4},{4,5},{5,6},{6,7},{7,0},{8,9},{9,10},{10,1... | collective-permute-start | bytes 786440 | tf_op jit(solution)/shard_map/ppermute | solution.py:243
  478.8 7.8 %collective-permute-start.7 = (bf16[64,2048]{1,0:T(8,128)(2,1)S(1)}, bf16[64,2048]{1,0:T(8,128)(2,1)S(1)}, u32[]{:S(2)}, u32[]{:S(2)}) collective-permute-start(bf16[64,2048]{1,0:T(8,128)(2,1)S(1)} %collective-permute-done.6), channel_id=1, source_target_pairs={{0,1},{1,2},{2,3},{3,4},{4,5},{5,6},{6,7},{7,0},{8,9},{9,10},{10,1... | collective-permute-start | bytes 786440 | tf_op jit(solution)/shard_map/ppermute | solution.py:243
  478.8 7.9 %collective-permute-start.10 = (bf16[64,2048]{1,0:T(8,128)(2,1)S(1)}, bf16[64,2048]{1,0:T(8,128)(2,1)S(1)}, u32[]{:S(2)}, u32[]{:S(2)}) collective-permute-start(bf16[64,2048]{1,0:T(8,128)(2,1)S(1)} %fusion.62), channel_id=1, source_target_pairs={{1,0},{2,1},{3,2},{4,3},{5,4},{6,5},{7,6},{0,7},{9,8},{10,9},{11,1... | collective-permute-start | bytes 786440 | tf_op jit(solution)/shard_map/ppermute | solution.py:246
  486.5 7.8 %collective-permute-start.8 = (bf16[64,2048]{1,0:T(8,128)(2,1)S(1)}, bf16[64,2048]{1,0:T(8,128)(2,1)S(1)}, u32[]{:S(2)}, u32[]{:S(2)}) collective-permute-start(bf16[64,2048]{1,0:T(8,128)(2,1)S(1)} %collective-permute-done.7), channel_id=1, source_target_pairs={{0,1},{1,2},{2,3},{3,4},{4,5},{5,6},{6,7},{7,0},{8,9},{9,10},{10,1... | collective-permute-start | bytes 786440 | tf_op jit(solution)/shard_map/ppermute | solution.py:243
  486.6 7.7 %collective-permute-start.11 = (bf16[64,2048]{1,0:T(8,128)(2,1)S(1)}, bf16[64,2048]{1,0:T(8,128)(2,1)S(1)}, u32[]{:S(2)}, u32[]{:S(2)}) collective-permute-start(bf16[64,2048]{1,0:T(8,128)(2,1)S(1)} %collective-permute-done.10), channel_id=1, source_target_pairs={{1,0},{2,1},{3,2},{4,3},{5,4},{6,5},{7,6},{0,7},{9,8},{10,9},{11,1... | collective-permute-start | bytes 786440 | tf_op jit(solution)/shard_map/ppermute | solution.py:246
  494.3 7.6 %collective-permute-start.9 = (bf16[64,2048]{1,0:T(8,128)(2,1)S(1)}, bf16[64,2048]{1,0:T(8,128)(2,1)S(1)}, u32[]{:S(2)}, u32[]{:S(2)}) collective-permute-start(bf16[64,2048]{1,0:T(8,128)(2,1)S(1)} %collective-permute-done.8), channel_id=1, source_target_pairs={{0,1},{1,2},{2,3},{3,4},{4,5},{5,6},{6,7},{7,0},{8,9},{9,10},{10,1... | collective-permute-start | bytes 786440 | tf_op jit(solution)/shard_map/ppermute | solution.py:243
  494.3 12.7 %collective-permute-start.12 = (bf16[64,2048]{1,0:T(8,128)(2,1)S(1)}, bf16[64,2048]{1,0:T(8,128)(2,1)S(1)}, u32[]{:S(2)}, u32[]{:S(2)}) collective-permute-start(bf16[64,2048]{1,0:T(8,128)(2,1)S(1)} %collective-permute-done.11), channel_id=1, source_target_pairs={{1,0},{2,1},{3,2},{4,3},{5,4},{6,5},{7,6},{0,7},{9,8},{10,9},{11,1... | collective-permute-start | bytes 786440 | tf_op jit(solution)/shard_map/ppermute | solution.py:246
  511.2 0.9 copy-start.14
  524.0 20.5 %copy-start.22 = (bf16[2048,8]{0,1:T(8,128)(2,1)S(1)}, bf16[2048,8]{0,1:T(8,128)(2,1)}, u32[]{:S(2)}) copy-start(bf16[2048,8]{0,1:T(8,128)(2,1)} %param.28) | copy-start | bytes 98308
  544.6 0.7 copy-start.18
  544.6 0.9 copy-start.20
  544.6 0.9 copy-start.25
  554.8 1.0 copy-start.9
  554.8 7.6 %copy-start.6 = (bf16[1,1024,512]{2,1,0:T(8,128)(2,1)S(1)}, bf16[1,1024,512]{2,1,0:T(8,128)(2,1)}, u32[]{:S(2)}) copy-start(bf16[1,1024,512]{2,1,0:T(8,128)(2,1)} %param.18) | copy-start | bytes 3145732
  558.0 32.7 %copy-start.1 = (bf16[2048,512]{1,0:T(8,128)(2,1)S(1)}, bf16[2048,512]{1,0:T(8,128)(2,1)}, u32[]{:S(2)}) copy-start(bf16[2048,512]{1,0:T(8,128)(2,1)} %param.25) | copy-start | bytes 6291460
Sparse Core Ops, SparseCore 0:
  11.0 34.2 all-gather.3
  433.8 35.7 reduce-scatter.2
  554.9 34.0 reduce-scatter.4
